TPU v7x, 32 devices: a whole 2x2x4 slice. The times are simulated.
32 devices in a mesh: win: 4 (over y, core), pair: 8 (over z, x).
Axes of the slice: x: 2, y: 2, z: 4, core: 2. Of those that a mesh axis runs over, the one named last changes fastest.
Arguments:
- strain: bfloat16 [4, 2048, 7680], P('win', 'pair'), may hold values from -40 to 40
- pair_list: int32 [32, 2], replicated, may hold values from 0 to 15, as said below
- tile_live: int32 [32], P('pair'), may hold values 0 or 1
Outputs:
- stack: float32 [128, 32, 16, 128], P('win', 'pair')
Inputs may be any that keep to these rules, and one draw needn't show every extreme that they name: `pair_list`: rows q * 4 to (q + 1) * 4 - 1 are the tiles of owner q; the 8 block numbers in them fall into distinct groups of 2 consecutive blocks.
All inputs are finite; a program needn't handle non-finite values. No bound on the sum of `tile_live` on one device may be relied on, other than what follows from the above.
Results may differ from a plain program's by a relative error of at most 0.02.
Values may be sent and summed in bfloat16 or wider, within the bound.
No kernel may reach another device: no remote copies, remote signals or barrier semaphores. Data moves between devices by JAX's collectives and lax.ppermute only.
A program may use at most 64 MiB of HBM per device.

v0:
```python
import math
import jax
import jax.numpy as jnp
from jax import lax
from jax.sharding import PartitionSpec as P

C = 128
F = 384
LAGS = 16
DECIM = 32
B_DEV = 2


def dft_piece(first_row, row_count, sample_count, bin_count):
    sample_index = first_row + lax.iota(jnp.int32, row_count)
    bin_index = lax.iota(jnp.int32, bin_count) + 1
    product = sample_index[:, None] * bin_index[None, :] % sample_count
    angle = 2.0 * math.pi / sample_count * product.astype(jnp.float32)
    return jnp.concatenate([jnp.cos(angle), -jnp.sin(angle)], axis=1).astype(jnp.bfloat16)


def lag_tables(sample_count, bin_count, lag_count, stride):
    bin_index = lax.iota(jnp.int32, bin_count) + 1
    lag_shift = (lax.iota(jnp.int32, lag_count) - lag_count // 2) * stride
    product = bin_index[:, None] * lag_shift[None, :] % sample_count
    angle = 2.0 * math.pi / sample_count * product.astype(jnp.float32)
    return (jnp.cos(angle), jnp.sin(angle))


def whiten_rows(strain_rows, bin_count):
    row_total, sample_count = strain_rows.shape
    piece_len = sample_count // 4
    spectrum = jnp.zeros((row_total, 2 * bin_count), jnp.float32)
    for piece_index in range(4):
        dft_table = dft_piece(piece_index * piece_len, piece_len, sample_count, bin_count)
        samples_part = strain_rows[:, piece_index * piece_len : (piece_index + 1) * piece_len]
        spectrum = spectrum + jnp.dot(samples_part, dft_table, preferred_element_type=jnp.float32)
    real_part = spectrum[:, :bin_count]
    imag_part = spectrum[:, bin_count:]
    amplitude = jnp.sqrt(real_part * real_part + imag_part * imag_part)
    level = 0.2 * jnp.mean(amplitude, axis=1, keepdims=True) + 1e-06
    divisor = jnp.maximum(amplitude, level)
    return jnp.concatenate([real_part / divisor, imag_part / divisor], axis=1).astype(jnp.bfloat16)


def shift_block(spectrum_block, cos_lag, sin_lag):
    bin_count = cos_lag.shape[0]
    real_part = spectrum_block[:, :bin_count].astype(jnp.float32).T
    imag_part = spectrum_block[:, bin_count:].astype(jnp.float32).T
    upper_half = (
        real_part[:, None, :] * cos_lag[:, :, None] + imag_part[:, None, :] * sin_lag[:, :, None]
    )
    lower_half = (
        imag_part[:, None, :] * cos_lag[:, :, None] - real_part[:, None, :] * sin_lag[:, :, None]
    )
    joined = jnp.concatenate([upper_half, lower_half], axis=0).astype(jnp.bfloat16)
    return joined.reshape(2 * bin_count, -1)


def body(strain, pair_list, tile_live):
    window_count, local_rows, sample_count = strain.shape
    slot_count = tile_live.shape[0]
    pair_here = lax.axis_index("pair")
    flat_rows = strain.reshape(window_count * local_rows, sample_count)
    whitened = whiten_rows(flat_rows, F).reshape(window_count, B_DEV, C, 2 * F)
    local_blocks = jnp.transpose(whitened, (1, 0, 2, 3))
    wanted = lax.dynamic_slice_in_dim(pair_list, pair_here * slot_count, slot_count, 0).reshape(
        2 * slot_count
    )
    blank_slots = jnp.zeros((2 * slot_count,) + local_blocks.shape[1:], jnp.bfloat16)
    shard_rows = lax.all_gather(local_blocks, "pair", axis=0, tiled=True)
    block_count = shard_rows.shape[0]
    inside = (wanted >= 0) & (wanted < block_count)
    picked = jnp.take(shard_rows, jnp.clip(wanted, 0, block_count - 1), axis=0)
    needed = jnp.where(inside[:, None, None, None], picked, blank_slots)
    cos_lag, sin_lag = lag_tables(sample_count, F, LAGS, DECIM)
    own_rows = C // lax.axis_size("win")
    results = []
    for slot_index in range(slot_count):
        shifted = shift_block(needed[2 * slot_index + 1, 0], cos_lag, sin_lag)
        left_rows = needed[2 * slot_index, 0]
        summed = jnp.dot(left_rows, shifted, preferred_element_type=jnp.float32)
        results.append(summed)
    stacked = lax.psum_scatter(
        jnp.stack(results, axis=1).astype(jnp.bfloat16), "win", scatter_dimension=0, tiled=True
    ).astype(jnp.float32)
    live_local = tile_live.astype(jnp.float32)
    output = (
        stacked * live_local[None, :, None] / math.sqrt(F * window_count * lax.axis_size("win"))
    )
    return output.reshape(own_rows, slot_count, LAGS, C)


def solution(mesh):
    in_specs = (P("win", "pair", None), P(), P("pair"))
    out_specs = P("win", "pair", None, None)
    return jax.shard_map(body, mesh=mesh, in_specs=in_specs, out_specs=out_specs, check_vma=False)
```

profile of v0, /device:TPU:0, one launch (start us, length us, event | category | flops | bytes accessed | tf_op | source)
XLA Modules:
  0.0 182.1 jit_solution(2870586868444226078)
XLA Ops:
  6.6 50.0 %cosine_convert_fusion = (bf16[1920,384]{1,0:T(8,128)(2,1)S(1)}, bf16[1920,384]{1,0:T(8,128)(2,1)S(1)}, bf16[1920,384]{1,0:T(8,128)(2,1)S(1)}, bf16[1920,384]{1,...) fusion(s32[1920]{0:T(1024)S(1)} %get-tuple-element.47, ...), kind=kLoop, calls=%fused_computation.54 | loop fusion | flops 35389440 | bytes 11821056 | tf_op jit(solution)/shard_map/convert.36
  56.6 1.0 fusion.24
  57.6 1.0 fusion.86
  58.6 1.0 fusion.83
  59.6 1.0 fusion.80
  60.6 0.2 fusion.109
  60.8 0.2 divide_convert_fusion.1
  61.0 0.8 pad_maximum_fusion.1
  61.8 0.2 reduce-scatter.2.cloned.1.call-start
  62.1 0.1 dynamic-slice_clamp_fusion
  62.1 0.1 copy.43
  62.2 0.1 min.18
  62.3 0.1 min.16
  62.5 0.1 copy.42
  62.6 0.1 and.81
  62.7 0.2 fusion.98
  62.9 0.1 copy.48
  63.0 0.1 copy.50
  63.2 61.9 %all-gather.2.cloned.1.call-done = bf16[16,1,128,768]{3,2,1,0:T(8,128)(2,1)} async-done(((bf16[2,1,128,768]{3,2,1,0:T(8,128)(2,1)}), bf16[16,1,128,768]{3,2,1,0:T(8,128)(2,1)}) %all-gather.2.cloned.1.call-update) | async-done | bytes 3145744 | tf_op jit(solution)/shard_map/all_gather | solution.py:71
  125.1 2.5 %gather_fusion = bf16[8,128,768]{2,1,0:T(8,128)(2,1)S(1)} fusion(bf16[16,128,768]{2,1,0:T(8,128)(2,1)} %bitcast.116, s32[1024]{0:T(1024)S(1)} %pad_clamp_fusion), kind=kCustom, calls=%fused_computation | custom fusion | bytes 3145760 | tf_op jit(solution)/shard_map/jit(_take)/gather | solution.py:74
  127.7 0.2 fusion.76
  128.0 0.1 copy.47
  128.1 0.1 copy.49
  128.3 0.1 copy.51
  128.4 0.1 copy.52
  128.6 0.1 copy.53
  128.7 0.1 copy.54
  128.9 0.7 convert_bitcast_fusion.1
  129.6 0.1 copy.55
  129.7 1.1 copy.56
  130.8 4.3 %add_convert_fusion.3 = (bf16[384,16,128]{2,1,0:T(8,128)(2,1)S(1)}, bf16[384,16,128]{2,1,0:T(8,128)(2,1)S(1)}, bf16[384,16,128]{2,1,0:T(8,128)(2,1)S(1)}, bf16[3...) fusion(f32[384,16]{1,0:T(8,128)S(1)} %copy.50, ...), kind=kLoop, calls=%fused_computation.28 | loop fusion | flops 25165824 | bytes 14204928 | tf_op jit(solution)/shard_map/convert.31
  135.0 0.4 copy.81
  135.5 0.4 copy.82
  135.9 0.4 copy.79
  136.3 0.4 copy.80
  136.7 0.4 copy.77
  137.1 0.4 copy.78
  137.5 0.4 copy.75
  138.0 0.4 copy.76
  138.4 0.6 fusion.64
  139.0 0.6 fusion.67
  139.6 0.6 fusion.70
  140.2 0.6 fusion.73
  140.9 1.6 pad_maximum_fusion
  142.5 30.2 %reduce-scatter.2.cloned.1.call-done = bf16[32,4,2048]{2,0,1:T(8,128)(2,1)} async-done(((bf16[128,4,2048]{2,0,1:T(8,128)(2,1)}), bf16[32,4,2048]{2,0,1:T(8,128)(2,1)}) %reduce-scatter.2.cloned.1.call-update) | async-done | bytes 524304 | tf_op jit(solution)/shard_map/reduce_scatter | solution.py:84
  172.7 1.2 multiply_multiply_fusion
  174.0 0.2 copy.66
  174.1 1.1 copy.57
  (23 shorter events, 0.3 us)
Async XLA Ops:
  6.5 118.6 %all-gather.2.cloned.1.call-start = ((), (), s32[]{:S(2)}) async-start(), calls=%async_computation.1 | async-start | bytes 3538944 | tf_op jit(solution)/shard_map/all_gather | solution.py:71
  6.6 50.1 %copy-start.1 = (bf16[1,256,7680]{2,1,0:T(8,128)(2,1)S(1)}, bf16[1,256,7680]{2,1,0:T(8,128)(2,1)}, u32[]{:S(2)}) copy-start(bf16[1,256,7680]{2,1,0:T(8,128)(2,1)} %param.3) | copy-start | bytes 11796484
  60.6 1.5 copy-start
  61.8 110.9 %reduce-scatter.2.cloned.1.call-start = ((), (), s32[]{:S(2)}) async-start(), calls=%async_computation.2 | async-start | bytes 2621440 | tf_op jit(solution)/shard_map/reduce_scatter | solution.py:84
  140.9 1.6 copy-start.2
Sparse Core Ops, SparseCore 0:
  61.9 63.1 all-gather.1
  142.6 30.0 reduce-scatter.1
where the time goes:
time: 182 us
  waiting for transfers between devices  92.1 us (51%)
  other arithmetic  59.8 us (33%)
  between operations  13.8 us (8%)
  local copies, waits for them, and re-layouts  9.81 us (5%)
  matrix products  6.39 us (4%)
    all_gather x1, waiting for transfers between devices, body(): shard_rows = lax.all_gather(local_blocks, 'pair', axis=0, tiled=True)  61.9 us
    another operation x3, other arithmetic  54.5 us
    reduce_scatter x1, waiting for transfers between devices, body(): lax.psum_scatter(jnp.stack(results, axis=1).astype(jnp.bfloat16), 'win',...  30.2 us
    dot_general x4, matrix products, whiten_rows(): jnp.dot(samples_part, dft_table, preferred_element_type=jnp.float32)  3.91 us
  transfers between devices with their start and end apart: 2, of which 2 were waited for; matrix products, arithmetic and copies ran while one was open for 1% of the time, Pallas kernels for 0%

commit v1 on v0

--- a/solution.py
+++ b/solution.py
@@ -68,7 +68,24 @@
         2 * slot_count
     )
     blank_slots = jnp.zeros((2 * slot_count,) + local_blocks.shape[1:], jnp.bfloat16)
-    shard_rows = lax.all_gather(local_blocks, "pair", axis=0, tiled=True)
+    ways, here, step = (lax.axis_size("pair"), lax.axis_index("pair"), local_blocks.shape[0])
+    shape = [n * ways if d == 0 else n for d, n in enumerate(local_blocks.shape)]
+    shard_rows = lax.dynamic_update_slice_in_dim(
+        jnp.zeros(shape, local_blocks.dtype), local_blocks, here * step, axis=0
+    )
+    going_up = going_down = local_blocks
+    for far in range(1, ways // 2 + 1):
+        going_up = lax.ppermute(going_up, "pair", [(d, (d + 1) % ways) for d in range(ways)])
+        shard_rows = lax.dynamic_update_slice_in_dim(
+            shard_rows, going_up, (here - far) % ways * step, axis=0
+        )
+        if 2 * far < ways:
+            going_down = lax.ppermute(
+                going_down, "pair", [(d, (d - 1) % ways) for d in range(ways)]
+            )
+            shard_rows = lax.dynamic_update_slice_in_dim(
+                shard_rows, going_down, (here + far) % ways * step, axis=0
+            )
     block_count = shard_rows.shape[0]
     inside = (wanted >= 0) & (wanted < block_count)
     picked = jnp.take(shard_rows, jnp.clip(wanted, 0, block_count - 1), axis=0)

time: 182 us -> 188 us (1.033)
  starting transfers between devices: 0.22 us -> 19.4 us
  waiting for transfers between devices: 92.1 us -> 74 us
  local copies, waits for them, and re-layouts: 9.81 us -> 13 us
    all_gather x1 -> x0, waiting for transfers between devices: 61.9 us -> none  [body(): shard_rows = lax.all_gather(local_blocks, 'pair', axis=0, tiled=True)]
    ppermute x0 -> x7, waiting for transfers between devices: none -> 43.9 us  [the longest x4 43.9 us: body(): lax.ppermute(going_up, 'pair', [(d, (d + 1) % ways) for d in range(ways)])]
    ppermute x0 -> x7, starting transfers between devices: none -> 19.4 us  [the longest x4 10.3 us: body(): lax.ppermute(going_up, 'pair', [(d, (d + 1) % ways) for d in range(ways)])]
    dynamic_update_slice x0 -> x8, local copies, waits for them, and re-layouts: none -> 2.51 us  [the longest x5 1.41 us: body(): lax.dynamic_update_slice_in_dim(shard_rows, going_up, (here - far) % ways...]
  transfers between devices with their start and end apart: 2 -> 8, of which waited for: 2 -> 5; matrix products, arithmetic and copies ran while one was open for 1% -> 3% of each run, Pallas kernels for 0% -> 0%
where the time goes in v1:
time: 188 us
  waiting for transfers between devices  74 us (39%)
  other arithmetic  61.3 us (33%)
  starting transfers between devices  19.4 us (10%)
  between operations  13.9 us (7%)
  local copies, waits for them, and re-layouts  13 us (7%)
  matrix products  6.4 us (3%)
    another operation x3, other arithmetic  54.5 us
    ppermute x4, waiting for transfers between devices, body(): lax.ppermute(going_up, 'pair', [(d, (d + 1) % ways) for d in range(ways)])  43.9 us
    reduce_scatter x1, waiting for transfers between devices, body(): lax.psum_scatter(jnp.stack(results, axis=1).astype(jnp.bfloat16), 'win',...  30.1 us
    ppermute x4, starting transfers between devices, body(): lax.ppermute(going_up, 'pair', [(d, (d + 1) % ways) for d in range(ways)])  10.3 us
    ppermute x3, starting transfers between devices, body(): lax.ppermute(going_down, 'pair', [(d, (d - 1) % ways) for d in range(ways)])  9.12 us
    dot_general x4, matrix products, whiten_rows(): jnp.dot(samples_part, dft_table, preferred_element_type=jnp.float32)  3.91 us
  transfers between devices with their start and end apart: 8, of which 5 were waited for; matrix products, arithmetic and copies ran while one was open for 3% of the time, Pallas kernels for 0%

profile of v1, /device:TPU:0, one launch (start us, length us, event | category | flops | bytes accessed | tf_op | source)
XLA Modules:
  0.0 188.0 jit_solution(1688008071248173882)
XLA Ops:
  6.6 50.1 %cosine_convert_fusion = (bf16[1920,384]{1,0:T(8,128)(2,1)S(1)}, bf16[1920,384]{1,0:T(8,128)(2,1)S(1)}, bf16[1920,384]{1,0:T(8,128)(2,1)S(1)}, bf16[1920,384]{1,...) fusion(s32[1920]{0:T(1024)S(1)} %get-tuple-element.47, ...), kind=kLoop, calls=%fused_computation.54 | loop fusion | flops 35389440 | bytes 11821056 | tf_op jit(solution)/shard_map/convert.36
  56.7 1.0 fusion.24
  57.6 1.0 fusion.86
  58.6 1.0 fusion.83
  59.6 1.0 fusion.80
  60.6 0.2 fusion.110
  60.8 0.2 divide_convert_fusion.1
  61.1 0.8 pad_maximum_fusion.1
  61.8 2.9 %collective-permute-start = (bf16[2,1,128,768]{3,2,0,1:T(8,128)(2,1)}, bf16[2,1,128,768]{3,2,0,1:T(8,128)(2,1)}, u32[]{:S(2)}, u32[]{:S(2)}) collective-permute-start(bf16[2,1,128,768]{3,2,0,1:T(8,128)(2,1)} %pad_maximum_fusion.1), channel_id=1, source_target_pairs={{0,1},{1,2},{2,3},{3,4},{4,5},{5,6},{6,7},{7,0},{8,9},{9,10},{10,1... | collective-permute-start | bytes 1179656 | tf_op jit(solution)/shard_map/ppermute | solution.py:78
  64.8 3.0 %collective-permute-start.1 = (bf16[2,1,128,768]{3,2,0,1:T(8,128)(2,1)}, bf16[2,1,128,768]{3,2,0,1:T(8,128)(2,1)}, u32[]{:S(2)}, u32[]{:S(2)}) collective-permute-start(bf16[2,1,128,768]{3,2,0,1:T(8,128)(2,1)} %pad_maximum_fusion.1), channel_id=1, source_target_pairs={{0,7},{1,0},{2,1},{3,2},{4,3},{5,4},{6,5},{7,6},{8,15},{9,8},{10,9... | collective-permute-start | bytes 1179656 | tf_op jit(solution)/shard_map/ppermute | solution.py:83
  68.1 0.2 fusion.98
  68.7 0.8 copy.24
  69.5 0.8 copy.26
  70.4 0.3 broadcast.304
  70.7 11.2 %collective-permute-done = bf16[2,1,128,768]{3,2,0,1:T(8,128)(2,1)} collective-permute-done((bf16[2,1,128,768]{3,2,0,1:T(8,128)(2,1)}, bf16[2,1,128,768]{3,2,0,1:T(8,128)(2,1)}, u32[]{:S(2)}, u32[]{:S(2)}) %collective-permute-start) | collective-permute-done | bytes 393248 | tf_op jit(solution)/shard_map/ppermute | solution.py:78
  81.9 2.5 %collective-permute-start.2 = (bf16[2,1,128,768]{3,2,0,1:T(8,128)(2,1)}, bf16[2,1,128,768]{3,2,0,1:T(8,128)(2,1)S(1)}, u32[]{:S(2)}, u32[]{:S(2)}) collective-permute-start(bf16[2,1,128,768]{3,2,0,1:T(8,128)(2,1)} %collective-permute-done), channel_id=1, source_target_pairs={{0,1},{1,2},{2,3},{3,4},{4,5},{5,6},{6,7},{7,0},{8,9},{9,10},{10,1... | collective-permute-start | bytes 1179656 | tf_op jit(solution)/shard_map/ppermute | solution.py:78
  84.4 3.0 %collective-permute-start.3 = (bf16[2,1,128,768]{3,2,0,1:T(8,128)(2,1)}, bf16[2,1,128,768]{3,2,0,1:T(8,128)(2,1)S(1)}, u32[]{:S(2)}, u32[]{:S(2)}) collective-permute-start(bf16[2,1,128,768]{3,2,0,1:T(8,128)(2,1)} %collective-permute-done.1), channel_id=1, source_target_pairs={{0,7},{1,0},{2,1},{3,2},{4,3},{5,4},{6,5},{7,6},{8,15},{9,8},{10,9... | collective-permute-start | bytes 1179656 | tf_op jit(solution)/shard_map/ppermute | solution.py:83
  87.4 1.0 bitcast_dynamic-update-slice_fusion.6
  88.4 1.0 bitcast_dynamic-update-slice_fusion.5
  89.5 11.1 %collective-permute-done.2 = bf16[2,1,128,768]{3,2,0,1:T(8,128)(2,1)S(1)} collective-permute-done((bf16[2,1,128,768]{3,2,0,1:T(8,128)(2,1)}, bf16[2,1,128,768]{3,2,0,1:T(8,128)(2,1)S(1)}, u32[]{:S(2)}, u32[]{:S(2)}) %collective-permute-start.2) | collective-permute-done | bytes 393248 | tf_op jit(solution)/shard_map/ppermute | solution.py:78
  100.6 2.4 %collective-permute-start.4 = (bf16[2,1,128,768]{3,2,0,1:T(8,128)(2,1)S(1)}, bf16[2,1,128,768]{3,2,0,1:T(8,128)(2,1)S(1)}, u32[]{:S(2)}, u32[]{:S(2)}) collective-permute-start(bf16[2,1,128,768]{3,2,0,1:T(8,128)(2,1)S(1)} %collective-permute-done.2), channel_id=1, source_target_pairs={{0,1},{1,2},{2,3},{3,4},{4,5},{5,6},{6,7},{7,0},{8,9},{9,10},{10,1... | collective-permute-start | bytes 1179656 | tf_op jit(solution)/shard_map/ppermute | solution.py:78
  103.0 3.0 %collective-permute-start.5 = (bf16[2,1,128,768]{3,2,0,1:T(8,128)(2,1)S(1)}, bf16[2,1,128,768]{3,2,0,1:T(8,128)(2,1)S(1)}, u32[]{:S(2)}, u32[]{:S(2)}) collective-permute-start(bf16[2,1,128,768]{3,2,0,1:T(8,128)(2,1)S(1)} %collective-permute-done.3), channel_id=1, source_target_pairs={{0,7},{1,0},{2,1},{3,2},{4,3},{5,4},{6,5},{7,6},{8,15},{9,8},{10,9... | collective-permute-start | bytes 1179656 | tf_op jit(solution)/shard_map/ppermute | solution.py:83
  106.1 12.0 %collective-permute-done.4 = bf16[2,1,128,768]{3,2,0,1:T(8,128)(2,1)S(1)} collective-permute-done((bf16[2,1,128,768]{3,2,0,1:T(8,128)(2,1)S(1)}, bf16[2,1,128,768]{3,2,0,1:T(8,128)(2,1)S(1)}, u32[]{:S(2)}, u32[]{:S(2)}) %collective-permute-start.4) | collective-permute-done | bytes 393248 | tf_op jit(solution)/shard_map/ppermute | solution.py:78
  118.1 2.5 %collective-permute-start.6 = (bf16[2,1,128,768]{3,2,0,1:T(8,128)(2,1)S(1)}, bf16[2,1,128,768]{3,2,0,1:T(8,128)(2,1)S(1)}, u32[]{:S(2)}, u32[]{:S(2)}) collective-permute-start(bf16[2,1,128,768]{3,2,0,1:T(8,128)(2,1)S(1)} %collective-permute-done.4), channel_id=1, source_target_pairs={{0,1},{1,2},{2,3},{3,4},{4,5},{5,6},{6,7},{7,0},{8,9},{9,10},{10,1... | collective-permute-start | bytes 1179656 | tf_op jit(solution)/shard_map/ppermute | solution.py:78
  120.7 9.6 %collective-permute-done.6 = bf16[2,1,128,768]{3,2,0,1:T(8,128)(2,1)S(1)} collective-permute-done((bf16[2,1,128,768]{3,2,0,1:T(8,128)(2,1)S(1)}, bf16[2,1,128,768]{3,2,0,1:T(8,128)(2,1)S(1)}, u32[]{:S(2)}, u32[]{:S(2)}) %collective-permute-start.6) | collective-permute-done | bytes 393248 | tf_op jit(solution)/shard_map/ppermute | solution.py:78
  130.3 1.8 gather_fusion
  132.1 1.6 fusion.76
  134.0 0.1 copy.25
  134.8 0.7 convert_bitcast_fusion.1
  135.6 1.1 copy.32
  136.7 4.3 %add_convert_fusion.3 = (bf16[384,16,128]{2,1,0:T(8,128)(2,1)S(1)}, bf16[384,16,128]{2,1,0:T(8,128)(2,1)S(1)}, bf16[384,16,128]{2,1,0:T(8,128)(2,1)S(1)}, bf16[3...) fusion(f32[384,16]{1,0:T(8,128)S(1)} %copy-done.1, ...), kind=kLoop, calls=%fused_computation.28 | loop fusion | flops 25165824 | bytes 14204928 | tf_op jit(solution)/shard_map/convert.31
  140.9 0.4 copy.57
  141.4 0.4 copy.58
  141.8 0.4 copy.55
  142.2 0.4 copy.56
  142.6 0.4 copy.53
  143.0 0.4 copy.54
  143.4 0.4 copy.51
  143.9 0.4 copy.52
  144.3 0.6 fusion.64
  144.9 0.6 fusion.67
  145.5 0.6 fusion.70
  146.2 0.6 fusion.73
  146.8 1.6 pad_maximum_fusion
  148.5 30.1 %reduce-scatter.2.cloned.1.call-done = bf16[32,4,2048]{2,0,1:T(8,128)(2,1)} async-done(((bf16[128,4,2048]{2,0,1:T(8,128)(2,1)}), bf16[32,4,2048]{2,0,1:T(8,128)(2,1)}) %reduce-scatter.2.cloned.1.call-update) | async-done | bytes 524304 | tf_op jit(solution)/shard_map/reduce_scatter | solution.py:101
  178.6 1.2 multiply_multiply_fusion
  179.8 0.2 copy.42
  180.0 1.1 copy.33
  (47 shorter events, 1.8 us)
Async XLA Ops:
  6.5 172.0 %reduce-scatter.2.cloned.1.call-start = ((), (), s32[]{:S(2)}) async-start(), calls=%async_computation.1 | async-start | bytes 2621440 | tf_op jit(solution)/shard_map/reduce_scatter | solution.py:101
  6.6 50.1 %copy-start.3 = (bf16[1,256,7680]{2,1,0:T(8,128)(2,1)S(1)}, bf16[1,256,7680]{2,1,0:T(8,128)(2,1)}, u32[]{:S(2)}) copy-start(bf16[1,256,7680]{2,1,0:T(8,128)(2,1)} %param.3) | copy-start | bytes 11796484
  59.6 8.2 %copy-start.2 = (s32[32,2]{0,1:T(2,128)S(1)}, s32[32,2]{0,1:T(2,128)}, u32[]{:S(2)}) copy-start(s32[32,2]{0,1:T(2,128)} %param.4) | copy-start | bytes 772
  61.8 20.1 %collective-permute-start = (bf16[2,1,128,768]{3,2,0,1:T(8,128)(2,1)}, bf16[2,1,128,768]{3,2,0,1:T(8,128)(2,1)}, u32[]{:S(2)}, u32[]{:S(2)}) collective-permute-start(bf16[2,1,128,768]{3,2,0,1:T(8,128)(2,1)} %pad_maximum_fusion.1), channel_id=1, source_target_pairs={{0,1},{1,2},{2,3},{3,4},{4,5},{5,6},{6,7},{7,0},{8,9},{9,10},{10,1... | collective-permute-start | bytes 1179656 | tf_op jit(solution)/shard_map/ppermute | solution.py:78
  64.8 19.6 %collective-permute-start.1 = (bf16[2,1,128,768]{3,2,0,1:T(8,128)(2,1)}, bf16[2,1,128,768]{3,2,0,1:T(8,128)(2,1)}, u32[]{:S(2)}, u32[]{:S(2)}) collective-permute-start(bf16[2,1,128,768]{3,2,0,1:T(8,128)(2,1)} %pad_maximum_fusion.1), channel_id=1, source_target_pairs={{0,7},{1,0},{2,1},{3,2},{4,3},{5,4},{6,5},{7,6},{8,15},{9,8},{10,9... | collective-permute-start | bytes 1179656 | tf_op jit(solution)/shard_map/ppermute | solution.py:83
  81.9 18.7 %collective-permute-start.2 = (bf16[2,1,128,768]{3,2,0,1:T(8,128)(2,1)}, bf16[2,1,128,768]{3,2,0,1:T(8,128)(2,1)S(1)}, u32[]{:S(2)}, u32[]{:S(2)}) collective-permute-start(bf16[2,1,128,768]{3,2,0,1:T(8,128)(2,1)} %collective-permute-done), channel_id=1, source_target_pairs={{0,1},{1,2},{2,3},{3,4},{4,5},{5,6},{6,7},{7,0},{8,9},{9,10},{10,1... | collective-permute-start | bytes 1179656 | tf_op jit(solution)/shard_map/ppermute | solution.py:78
  84.4 18.6 %collective-permute-start.3 = (bf16[2,1,128,768]{3,2,0,1:T(8,128)(2,1)}, bf16[2,1,128,768]{3,2,0,1:T(8,128)(2,1)S(1)}, u32[]{:S(2)}, u32[]{:S(2)}) collective-permute-start(bf16[2,1,128,768]{3,2,0,1:T(8,128)(2,1)} %collective-permute-done.1), channel_id=1, source_target_pairs={{0,7},{1,0},{2,1},{3,2},{4,3},{5,4},{6,5},{7,6},{8,15},{9,8},{10,9... | collective-permute-start | bytes 1179656 | tf_op jit(solution)/shard_map/ppermute | solution.py:83
  100.6 17.5 %collective-permute-start.4 = (bf16[2,1,128,768]{3,2,0,1:T(8,128)(2,1)S(1)}, bf16[2,1,128,768]{3,2,0,1:T(8,128)(2,1)S(1)}, u32[]{:S(2)}, u32[]{:S(2)}) collective-permute-start(bf16[2,1,128,768]{3,2,0,1:T(8,128)(2,1)S(1)} %collective-permute-done.2), channel_id=1, source_target_pairs={{0,1},{1,2},{2,3},{3,4},{4,5},{5,6},{6,7},{7,0},{8,9},{9,10},{10,1... | collective-permute-start | bytes 1179656 | tf_op jit(solution)/shard_map/ppermute | solution.py:78
  103.0 17.7 %collective-permute-start.5 = (bf16[2,1,128,768]{3,2,0,1:T(8,128)(2,1)S(1)}, bf16[2,1,128,768]{3,2,0,1:T(8,128)(2,1)S(1)}, u32[]{:S(2)}, u32[]{:S(2)}) collective-permute-start(bf16[2,1,128,768]{3,2,0,1:T(8,128)(2,1)S(1)} %collective-permute-done.3), channel_id=1, source_target_pairs={{0,7},{1,0},{2,1},{3,2},{4,3},{5,4},{6,5},{7,6},{8,15},{9,8},{10,9... | collective-permute-start | bytes 1179656 | tf_op jit(solution)/shard_map/ppermute | solution.py:83
  118.1 12.1 %collective-permute-start.6 = (bf16[2,1,128,768]{3,2,0,1:T(8,128)(2,1)S(1)}, bf16[2,1,128,768]{3,2,0,1:T(8,128)(2,1)S(1)}, u32[]{:S(2)}, u32[]{:S(2)}) collective-permute-start(bf16[2,1,128,768]{3,2,0,1:T(8,128)(2,1)S(1)} %collective-permute-done.4), channel_id=1, source_target_pairs={{0,1},{1,2},{2,3},{3,4},{4,5},{5,6},{6,7},{7,0},{8,9},{9,10},{10,1... | collective-permute-start | bytes 1179656 | tf_op jit(solution)/shard_map/ppermute | solution.py:78
  133.8 2.8 %copy-start = (f32[384,16]{1,0:T(8,128)S(1)}, f32[384,16]{1,0:T(8,128)}, u32[]{:S(2)}) copy-start(f32[384,16]{1,0:T(8,128)} %copy.24) | copy-start | bytes 73732
  133.8 2.8 %copy-start.1 = (f32[384,16]{1,0:T(8,128)S(1)}, f32[384,16]{1,0:T(8,128)}, u32[]{:S(2)}) copy-start(f32[384,16]{1,0:T(8,128)} %copy.26) | copy-start | bytes 73732
  146.8 1.6 copy-start.4
Sparse Core Ops, SparseCore 0:
  148.6 29.9 reduce-scatter.1
